TPU v7x, 256 devices: a whole 4x4x8 slice. The times are simulated.
256 devices in a mesh: act: 32 (over x, y, core), pix: 8 (over z).
Axes of the slice: x: 4, y: 4, z: 8, core: 2. Of those that a mesh axis runs over, the one named last changes fastest.
Arguments:
- pixel_index: int32 [8, 512], P('pix'), may hold values from 0 to 65535
- act_map: int32 [32768], P('act'), may hold values from 0 to 32767, each once
- omega: bfloat16 [32768, 128], P('act'), may hold values from -6 to 6
- pupil_field: float32 [8, 2, 32768], P('pix', None, 'act'), may hold values from -6 to 6
- channel_scale: float32 [8], P('pix'), may hold values from 0.9 to 1.1
- channel_flux: float32 [8], P('pix'), may hold values from 0.3 to 3
Outputs:
- basis_out: float32 [8, 1024, 128], P('pix', 'act')
- projection: float32 [128, 32768], P('pix', 'act')
- r_factor: float32 [128, 128], replicated
Inputs may be any that keep to these rules, and one draw needn't show every extreme that they name: `act_map`: every number of 0 to 32767 appears once. `pixel_index`: pixels of a channel may repeat.
All inputs are finite; a program needn't handle non-finite values.
Results may differ from a plain program's by a relative error of at most 0.0048.
Values may be sent and summed in bfloat16 or wider, within the bound.
No kernel may reach another device: no remote copies, remote signals or barrier semaphores. Data moves between devices by JAX's collectives and lax.ppermute only.
A program may use at most 64 MiB of HBM per device.

v0:
```python
import math
import jax
import jax.numpy as jnp
from jax import lax
from jax.sharding import PartitionSpec as P

GRID = 128
FOCAL = 256
RANK = 128
ACT = 32768
TWO_PI = 2.0 * math.pi
INFL_RATE = 4.5
DEFOCUS_RATE = 6.0


def jacobian_planes(pixels, wave_scale, flux_level, codes, field_re, field_im):
    delta_u = pixels // FOCAL - FOCAL // 2
    delta_v = pixels % FOCAL - FOCAL // 2
    mirror = codes // (GRID * GRID)
    column_x = codes // GRID % GRID - GRID // 2
    column_y = codes % GRID - GRID // 2
    phase_int = delta_u[:, None] * column_x[None, :] + delta_v[:, None] * column_y[None, :]
    radius = (delta_u * delta_u + delta_v * delta_v).astype(jnp.float32)
    amplitude = flux_level * jnp.exp(-INFL_RATE * radius / (FOCAL * FOCAL))
    defocus = radius * (TWO_PI * DEFOCUS_RATE / (FOCAL * FOCAL)) / wave_scale
    phase_angle = mirror.astype(jnp.float32)[None, :] * defocus[
        :, None
    ] - TWO_PI / FOCAL * wave_scale * phase_int.astype(jnp.float32)
    cosine = jnp.cos(phase_angle)
    sine_part = jnp.sin(phase_angle)
    real_part = amplitude[:, None] * (field_re[None, :] * cosine - field_im[None, :] * sine_part)
    imag_part = amplitude[:, None] * (field_re[None, :] * sine_part + field_im[None, :] * cosine)
    return (real_part.astype(jnp.bfloat16), imag_part.astype(jnp.bfloat16))


def gram_of(sketch):
    return lax.dot_general(
        sketch,
        sketch,
        (((0,), (0,)), ((), ())),
        precision=lax.Precision.HIGHEST,
        preferred_element_type=jnp.float32,
    )


def on_device(pixel_index, act_map, omega, pupil_field, channel_scale, channel_flux):
    pixels = pixel_index[0]
    npix = pixels.shape[0]
    rows_dev = 2 * npix
    act_count = lax.axis_size("act")
    pix_count = lax.axis_size("pix")
    total_rows = rows_dev * pix_count
    share_pix = npix // act_count
    real_rows, imag_rows = jacobian_planes(
        pixels, channel_scale[0], channel_flux[0], act_map, pupil_field[0, 0], pupil_field[0, 1]
    )
    jac = jnp.concatenate([real_rows, imag_rows], axis=0)
    partial_sketch = jnp.dot(jac, omega, preferred_element_type=jnp.float32)
    sketch = lax.psum(partial_sketch, "act")
    gram_matrix = lax.psum(gram_of(sketch), "pix")
    lower_factor = jnp.linalg.cholesky(gram_matrix)
    basis = jax.scipy.linalg.solve_triangular(lower_factor, sketch.T, lower=True).T
    first = lax.axis_index("act") * share_pix
    own_re = lax.dynamic_slice_in_dim(basis, first, share_pix, 0)
    own_im = lax.dynamic_slice_in_dim(basis, npix + first, share_pix, 0)
    own_basis = jnp.stack([own_re, own_im], axis=1).reshape(2 * share_pix, RANK)
    coarse = basis.astype(jnp.bfloat16)
    partial_value = lax.dot_general(
        coarse, jac, (((0,), (0,)), ((), ())), preferred_element_type=jnp.float32
    )
    projection = lax.psum_scatter(partial_value, "pix", scatter_dimension=0, tiled=True)
    basis_out = (own_basis * math.sqrt(total_rows)).reshape(1, 2 * share_pix, RANK)
    r_factor = lower_factor.T / math.sqrt(total_rows * ACT)
    return (basis_out, projection, r_factor)


def solution(mesh):
    return jax.shard_map(
        on_device,
        mesh=mesh,
        in_specs=(
            P("pix", None),
            P("act"),
            P("act", None),
            P("pix", None, "act"),
            P("pix"),
            P("pix"),
        ),
        out_specs=(P("pix", "act", None), P("pix", "act"), P()),
        check_vma=False,
    )
```

profile of v0, /device:TPU:2, one launch (start us, length us, event | category | flops | bytes accessed | tf_op | source)
XLA Modules:
  0.0 285.0 jit_solution(6364925790602597482)
XLA Ops:
  7.2 0.0 all-reduce.3.cloned.1.call-start
  7.9 0.7 fusion.16
  8.6 0.7 exponential_multiply_fusion
  10.0 0.7 fusion.9
  10.7 0.8 fusion.21
  11.4 0.7 multiply_divide_fusion
  12.1 9.1 %multiply_convert_fusion.1 = (bf16[512,1024]{1,0:T(8,128)(2,1)S(1)}, bf16[512,1024]{1,0:T(8,128)(2,1)S(1)}) fusion(f32[1024]{0:T(1024)S(1)} %bitcast.32, s32[1024]{0:T(1024)S(1)} %get-tuple-element.17, s32[512]{0:T(512)S(1)} %fusion.16, s32[1024]{0:T(1024)S(1)} %get-tuple-element.18, s32[512]{0:T(512)S(1)} %get-tuple-element.7, f32[]{:T(128)S(6)} %mul_shard_map.3, ...), kind=kLoop, calls=%fused_computation.2 | loop fusion | flops 8912896 | bytes 2125828 | tf_op jit(solution)/shard_map/convert_element_type | solution.py:33
  21.2 1.5 fusion.3
  22.8 0.0 all-reduce.5.cloned.1.call-start
  22.8 116.9 %all-reduce.3.cloned.1.call-done = f32[1024,128]{1,0:T(8,128)} async-done(((f32[1024,128]{1,0:T(8,128)}), f32[1024,128]{1,0:T(8,128)}) %all-reduce.3.cloned.1.call-update) | async-done | bytes 524304 | tf_op jit(solution)/shard_map/psum | solution.py:59
  139.7 2.9 %fusion.22 = f32[128,128]{0,1:T(8,128)} fusion(f32[1024,128]{1,0:T(8,128)} %all-reduce.3.cloned.1.call-done), kind=kOutput, calls=%fused_computation.58 | convolution fusion | flops 201326592 | bytes 589824 | tf_op jit(solution)/shard_map/dot_general | solution.py:37
  142.7 0.0 reduce-scatter.2.cloned.1.call-start
  142.7 72.8 %all-reduce.5.cloned.1.call-done = f32[128,128]{0,1:T(8,128)} async-done(((f32[128,128]{0,1:T(8,128)}), f32[128,128]{0,1:T(8,128)}) %all-reduce.5.cloned.1.call-update) | async-done | bytes 65552 | tf_op jit(solution)/shard_map/psum | solution.py:60
  215.5 0.9 copy.10
  216.4 0.9 fusion.7
  217.3 11.7 %cholesky.16 = f32[128,128]{1,0:T(8,128)S(1)} custom-call(f32[128,128]{1,0:T(8,128)S(1)} %fusion.7), custom_call_target="Cholesky" | custom-call | tf_op jit(solution)/shard_map/jit(cholesky)/cholesky | solution.py:61
  229.0 0.6 compare_reduce_fusion
  229.7 0.7 multiply_bitcast_fusion
  230.3 9.8 %custom-call.7 = f32[1,128,128]{1,2,0:T(8,128)S(1)} custom-call(f32[1,128,128]{2,1,0:T(8,128)S(1)} %get-tuple-element.11), custom_call_target="InvertDiagBlocksLowerTriangular" | custom-call | tf_op jit(solution)/shard_map/jit(_solve_triangular)/triangular_solve | solution.py:62
  240.1 0.6 fusion.5
  240.7 1.3 fusion.2
  242.0 0.7 copy.11
  242.7 0.6 maximum_multiply_fusion
  243.4 35.1 %reduce-scatter.2.cloned.1.call-done = f32[16,1024]{1,0:T(8,128)} async-done(((f32[128,1024]{1,0:T(8,128)}), f32[16,1024]{1,0:T(8,128)}) %reduce-scatter.2.cloned.1.call-update) | async-done | bytes 65552 | tf_op jit(solution)/shard_map/reduce_scatter | solution.py:71
  (9 shorter events, 0.1 us)
Async XLA Ops:
  7.2 14.1 %copy-start = (bf16[1024,128]{1,0:T(8,128)(2,1)S(1)}, bf16[1024,128]{1,0:T(8,128)(2,1)}, u32[]{:S(2)}) copy-start(bf16[1024,128]{1,0:T(8,128)(2,1)} %param.8) | copy-start | bytes 786436
  7.2 132.6 %all-reduce.3.cloned.1.call-start = ((), (), s32[]{:S(2)}) async-start(), calls=%async_computation.1 | async-start | bytes 1048576 | tf_op jit(solution)/shard_map/psum | solution.py:59
  22.8 192.7 %all-reduce.5.cloned.1.call-start = ((), (), s32[]{:S(2)}) async-start(), calls=%async_computation.2 | async-start | bytes 131072 | tf_op jit(solution)/shard_map/psum | solution.py:60
  139.7 100.4 %copy-start.1 = (f32[1024,128]{1,0:T(8,128)S(1)}, f32[1024,128]{1,0:T(8,128)}, u32[]{:S(2)}) copy-start(f32[1024,128]{1,0:T(8,128)} %all-reduce.3.cloned.1.call-done) | copy-start | bytes 1572868
  142.7 135.8 %reduce-scatter.2.cloned.1.call-start = ((), (), s32[]{:S(2)}) async-start(), calls=%async_computation.3 | async-start | bytes 589824 | tf_op jit(solution)/shard_map/reduce_scatter | solution.py:71
Sparse Core Ops, SparseCore 0:
  22.9 116.8 all-reduce.2
  142.8 72.6 all-reduce.4
  242.1 36.2 reduce-scatter.1
where the time goes:
time: 285 us
  waiting for transfers between devices  225 us (79%)
  other arithmetic  36.2 us (13%)
  between operations  15.2 us (5%)
  matrix products  6.22 us (2%)
    psum x1, waiting for transfers between devices, on_device(): sketch = lax.psum(partial_sketch, 'act')  117 us
    psum x1, waiting for transfers between devices, on_device(): gram_matrix = lax.psum(gram_of(sketch), 'pix')  72.8 us
    reduce_scatter x1, waiting for transfers between devices, on_device(): lax.psum_scatter(partial_value, 'pix', scatter_dimension=0, tiled=True)  35.1 us
    another operation x3, other arithmetic, on_device(): lower_factor = jnp.linalg.cholesky(gram_matrix)  12.4 us
    another operation x1, other arithmetic, on_device(): jax.scipy.linalg.solve_triangular(lower_factor, sketch.T, lower=True)  9.81 us
    convert_element_type x1, other arithmetic, jacobian_planes(): return (real_part.astype(jnp.bfloat16), imag_part.astype(jnp.bfloat16))  9.06 us
  transfers between devices with their start and end apart: 3, of which 3 were waited for; matrix products, arithmetic and copies ran while one was open for 0% of the time, Pallas kernels for 0%

commit v1 on v0

--- a/solution.py
+++ b/solution.py
@@ -57,7 +57,7 @@
     jac = jnp.concatenate([real_rows, imag_rows], axis=0)
     partial_sketch = jnp.dot(jac, omega, preferred_element_type=jnp.float32)
     sketch = lax.psum(partial_sketch, "act")
-    gram_matrix = lax.psum(gram_of(sketch), "pix")
+    gram_matrix = jnp.sum(lax.all_gather(gram_of(sketch), "pix"), axis=0)
     lower_factor = jnp.linalg.cholesky(gram_matrix)
     basis = jax.scipy.linalg.solve_triangular(lower_factor, sketch.T, lower=True).T
     first = lax.axis_index("act") * share_pix

time: 285 us -> 237 us (0.83)
  waiting for transfers between devices: 225 us -> 152 us
  blocking collectives: 0 us -> 27.2 us
    psum x1 -> x0, waiting for transfers between devices: 72.8 us -> none  [on_device(): gram_matrix = lax.psum(gram_of(sketch), 'pix')]
    all_gather x0 -> x1, blocking collectives: none -> 27.2 us  [on_device(): gram_matrix = jnp.sum(lax.all_gather(gram_of(sketch), 'pix'), axis=0)]
  transfers between devices with their start and end apart: 3 -> 2, of which waited for: 3 -> 2; matrix products, arithmetic and copies ran while one was open for 0% -> 1% of each run, Pallas kernels for 0% -> 0%
where the time goes in v1:
time: 237 us
  waiting for transfers between devices  152 us (64%)
  other arithmetic  35.4 us (15%)
  blocking collectives  27.2 us (11%)
  between operations  15.5 us (7%)
  matrix products  5.54 us (2%)
    psum x1, waiting for transfers between devices, on_device(): sketch = lax.psum(partial_sketch, 'act')  117 us
    reduce_scatter x1, waiting for transfers between devices, on_device(): lax.psum_scatter(partial_value, 'pix', scatter_dimension=0, tiled=True)  34.8 us
    all_gather x1, blocking collectives, on_device(): gram_matrix = jnp.sum(lax.all_gather(gram_of(sketch), 'pix'), axis=0)  27.2 us
    another operation x3, other arithmetic, on_device(): lower_factor = jnp.linalg.cholesky(gram_matrix)  12.4 us
    another operation x1, other arithmetic, on_device(): jax.scipy.linalg.solve_triangular(lower_factor, sketch.T, lower=True)  9.81 us
    convert_element_type x1, other arithmetic, jacobian_planes(): return (real_part.astype(jnp.bfloat16), imag_part.astype(jnp.bfloat16))  9.06 us
  transfers between devices with their start and end apart: 2, of which 2 were waited for; matrix products, arithmetic and copies ran while one was open for 1% of the time, Pallas kernels for 0%

profile of v1, /device:TPU:2, one launch (start us, length us, event | category | flops | bytes accessed | tf_op | source)
XLA Modules:
  0.0 237.0 jit_solution(5964137047698215966)
XLA Ops:
  7.2 0.0 all-reduce.2.cloned.1.call-start
  7.9 0.7 fusion.16
  8.6 0.7 exponential_multiply_fusion
  10.0 0.7 fusion.9
  10.7 0.8 fusion.21
  11.4 0.7 multiply_divide_fusion
  12.1 9.1 %multiply_convert_fusion.1 = (bf16[512,1024]{1,0:T(8,128)(2,1)S(1)}, bf16[512,1024]{1,0:T(8,128)(2,1)S(1)}) fusion(f32[1024]{0:T(1024)S(1)} %bitcast.34, s32[1024]{0:T(1024)S(1)} %get-tuple-element.20, s32[512]{0:T(512)S(1)} %fusion.16, s32[1024]{0:T(1024)S(1)} %get-tuple-element.21, s32[512]{0:T(512)S(1)} %get-tuple-element.10, f32[]{:T(128)S(6)} %mul_shard_map.3, ...), kind=kLoop, calls=%fused_computation.2 | loop fusion | flops 8912896 | bytes 2125828 | tf_op jit(solution)/shard_map/convert_element_type | solution.py:33
  21.2 1.5 fusion.3
  22.7 0.0 all-reduce.2.cloned.1.call-update
  22.8 0.0 reduce-scatter.2.cloned.1.call-start
  22.8 116.9 %all-reduce.2.cloned.1.call-done = f32[1024,128]{1,0:T(8,128)} async-done(((f32[1024,128]{1,0:T(8,128)}), f32[1024,128]{1,0:T(8,128)}) %all-reduce.2.cloned.1.call-update) | async-done | bytes 524304 | tf_op jit(solution)/shard_map/psum | solution.py:59
  139.7 2.2 fusion.22
  142.0 27.2 %all-gather = f32[1024,128]{1,0:T(8,128)S(1)} all-gather(f32[128,128]{1,0:T(8,128)S(1)} %fusion.22), channel_id=2, replica_groups=mesh['act'=32,'pix'=8] {'pix'}, dimensions={0}, use_global_device_ids=true | all-gather | bytes 589824 | tf_op jit(solution)/shard_map/all_gather | solution.py:60
  169.2 0.1 copy.11
  169.3 11.7 %cholesky.16 = f32[128,128]{1,0:T(8,128)S(1)} custom-call(f32[128,128]{1,0:T(8,128)S(1)} %fusion.7), custom_call_target="Cholesky" | custom-call | tf_op jit(solution)/shard_map/jit(cholesky)/cholesky | solution.py:61
  181.1 0.6 compare_reduce_fusion
  181.7 0.7 multiply_bitcast_fusion
  182.4 9.8 %custom-call.7 = f32[1,128,128]{1,2,0:T(8,128)S(1)} custom-call(f32[1,128,128]{2,1,0:T(8,128)S(1)} %get-tuple-element.14), custom_call_target="InvertDiagBlocksLowerTriangular" | custom-call | tf_op jit(solution)/shard_map/jit(_solve_triangular)/triangular_solve | solution.py:62
  192.2 0.6 fusion.5
  192.8 1.3 fusion.2
  194.0 0.0 reduce-scatter.2.cloned.1.call-update
  194.1 0.7 copy.12
  194.8 0.6 maximum_multiply_fusion
  195.4 34.8 %reduce-scatter.2.cloned.1.call-done = f32[16,1024]{1,0:T(8,128)} async-done(((f32[128,1024]{1,0:T(8,128)}), f32[16,1024]{1,0:T(8,128)}) %reduce-scatter.2.cloned.1.call-update) | async-done | bytes 65552 | tf_op jit(solution)/shard_map/reduce_scatter | solution.py:71
  (8 shorter events, 0.1 us)
Async XLA Ops:
  7.2 14.1 %copy-start = (bf16[1024,128]{1,0:T(8,128)(2,1)S(1)}, bf16[1024,128]{1,0:T(8,128)(2,1)}, u32[]{:S(2)}) copy-start(bf16[1024,128]{1,0:T(8,128)(2,1)} %param.8) | copy-start | bytes 786436
  7.2 132.6 %all-reduce.2.cloned.1.call-start = ((), (), s32[]{:S(2)}) async-start(), calls=%async_computation.1 | async-start | bytes 1048576 | tf_op jit(solution)/shard_map/psum | solution.py:59
  22.8 207.4 %reduce-scatter.2.cloned.1.call-start = ((), (), s32[]{:S(2)}) async-start(), calls=%async_computation.2 | async-start | bytes 589824 | tf_op jit(solution)/shard_map/reduce_scatter | solution.py:71
  141.9 50.2 %copy-start.1 = (f32[1024,128]{1,0:T(8,128)S(1)}, f32[1024,128]{1,0:T(8,128)}, u32[]{:S(2)}) copy-start(f32[1024,128]{1,0:T(8,128)} %all-reduce.2.cloned.1.call-done) | copy-start | bytes 1572868
Sparse Core Ops, SparseCore 0:
  22.9 116.8 all-reduce.1
  194.2 35.9 reduce-scatter.1
